TPU v7x, 128 devices: a whole 4x4x4 slice. The times are simulated.
128 devices in a mesh: sub: 128 (over z, y, x, core).
Axes of the slice: x: 4, y: 4, z: 4, core: 2. Of those that a mesh axis runs over, the one named last changes fastest.
Arguments:
- pool_inputs: bfloat16 [65536, 4096], P('sub'), may hold values from -6 to 6
- pool_targets: bfloat16 [65536, 4096], P('sub'), may hold values from -6 to 6
- row_picks: int32 [8, 32768], P(None, 'sub'), may hold values from 0 to 511
- weight_in: float32 [4096, 32768], P(None, 'sub'), may hold values from -6 to 6
- weight_out: float32 [4096, 32768], P(None, 'sub'), may hold values from -6 to 6
- eval_inputs: bfloat16 [256, 4096], P('sub'), may hold values from -6 to 6
- handover: int32 [4096], replicated, may hold values from 0 to 4095, as said below
Outputs:
- trained_in: float32 [4096, 32768], P(None, 'sub')
- trained_out: float32 [4096, 32768], P(None, 'sub')
- prediction: float32 [256, 4096], P('sub')
Inputs may be any that keep to these rules, and one draw needn't show every extreme that they name: `row_picks`: indices into the subnet's own 512 resident rows. handover[g] is the new position of neuron group g (neurons 8 g to 8 g + 7); every position is taken once, and no two groups of one subnet move to the same subnet.
All inputs are finite; a program needn't handle non-finite values.
Results may differ from a plain program's by a relative error of at most 0.0065.
Values may be sent and summed in bfloat16 or wider, within the bound.
No kernel may reach another device: no remote copies, remote signals or barrier semaphores. Data moves between devices by JAX's collectives and lax.ppermute only.
A program may use at most 192 MiB of HBM per device.

v0:
```python
import math
import jax
import jax.numpy as jnp
from jax import lax
from jax.sharding import PartitionSpec as P

D = 4096
GROUP = 8
STEPS = 4
tanh_coef = 0.7978845608028654
cubic_coef = 0.044715
step_rate = 0.5


def gelu_value(inputs):
    inner_term = tanh_coef * (inputs + cubic_coef * inputs * inputs * inputs)
    return 0.5 * inputs * (1.0 + jnp.tanh(inner_term))


def gelu_parts(inputs):
    tanh_part = jnp.tanh(tanh_coef * (inputs + cubic_coef * inputs * inputs * inputs))
    values = 0.5 * inputs * (1.0 + tanh_part)
    slopes = 0.5 * (1.0 + tanh_part) + 0.5 * inputs * (1.0 - tanh_part * tanh_part) * tanh_coef * (
        1.0 + 3.0 * cubic_coef * inputs * inputs
    )
    return (values, slopes)


def train_step(layer_in, layer_out, batch_rows, batch_goals, scale_in, scale_out):
    in_half = layer_in.astype(jnp.bfloat16)
    out_half = layer_out.astype(jnp.bfloat16)
    before = jnp.dot(batch_rows, in_half, preferred_element_type=jnp.float32) * scale_in
    values, slopes = gelu_parts(before)
    activity = values.astype(jnp.bfloat16)
    branch = jnp.dot(activity, out_half.T, preferred_element_type=jnp.float32) * scale_out
    errors = (branch - batch_goals.astype(jnp.float32)).astype(jnp.bfloat16)
    grad_out = jnp.dot(errors.T, activity, preferred_element_type=jnp.float32) * scale_out
    backward = (
        jnp.dot(errors, out_half, preferred_element_type=jnp.float32) * scale_out * slopes
    ).astype(jnp.bfloat16)
    grad_in = jnp.dot(batch_rows.T, backward, preferred_element_type=jnp.float32) * scale_in
    return (layer_in - step_rate * grad_in, layer_out - step_rate * grad_out)


def local_round(
    layer_in, layer_out, pool_inputs, pool_targets, row_picks, first_turn, scale_in, scale_out
):

    def one_turn(turn_index, carry):
        current_in, current_out = carry
        picked = lax.dynamic_slice_in_dim(row_picks, first_turn + turn_index, 1, 0)[0]
        batch_rows = jnp.take(pool_inputs, picked, axis=0)
        batch_goals = jnp.take(pool_targets, picked, axis=0)
        return train_step(current_in, current_out, batch_rows, batch_goals, scale_in, scale_out)

    return lax.fori_loop(0, STEPS, one_turn, (layer_in, layer_out))


def per_device(pool_inputs, pool_targets, row_picks, weight_in, weight_out, eval_inputs, handover):
    owners = lax.axis_size("sub")
    my_index = lax.axis_index("sub")
    hidden = weight_in.shape[1]
    group_count = hidden // GROUP
    total_groups = group_count * owners
    scale_in = 1.0 / math.sqrt(D)
    scale_out = 1.0 / math.sqrt(hidden * owners)
    layer_in, layer_out = local_round(
        weight_in, weight_out, pool_inputs, pool_targets, row_picks, 0, scale_in, scale_out
    )
    in_half = layer_in.astype(jnp.bfloat16)
    out_half = layer_out.astype(jnp.bfloat16)
    eval_act = gelu_value(
        jnp.dot(
            lax.all_gather(eval_inputs, "sub", axis=0, tiled=True),
            in_half,
            preferred_element_type=jnp.float32,
        )
        * scale_in
    ).astype(jnp.bfloat16)
    prediction = lax.psum_scatter(
        jnp.dot(eval_act, out_half.T, preferred_element_type=jnp.float32) * scale_out,
        "sub",
        scatter_dimension=0,
        tiled=True,
    )
    inverse = (
        jnp.zeros((total_groups,), jnp.int32)
        .at[handover]
        .set(jnp.arange(total_groups, dtype=jnp.int32))
    )
    offsets = jnp.arange(GROUP, dtype=jnp.int32)
    local_groups = lax.dynamic_slice_in_dim(handover, my_index * group_count, group_count, 0)
    targets = local_groups // group_count
    matches = targets[None, :] == jnp.arange(owners, dtype=jnp.int32)[:, None]
    chosen_group = jnp.sum(
        jnp.where(matches, jnp.arange(group_count, dtype=jnp.int32)[None, :], 0), axis=1
    )
    send_columns = (chosen_group[:, None] * GROUP + offsets[None, :]).reshape(-1)
    outgoing_in = jnp.take(layer_in, send_columns, axis=1)
    outgoing_out = jnp.take(layer_out, send_columns, axis=1)
    landed_in, landed_out = (
        lax.all_to_all(outgoing_in, "sub", split_axis=1, concat_axis=1, tiled=True),
        lax.all_to_all(outgoing_out, "sub", split_axis=1, concat_axis=1, tiled=True),
    )
    arriving = lax.dynamic_slice_in_dim(inverse, my_index * group_count, group_count, 0)
    sources = arriving // group_count
    take_columns = (sources[:, None] * GROUP + offsets[None, :]).reshape(-1)
    handed_in = jnp.take(landed_in, take_columns, axis=1)
    handed_out = jnp.take(landed_out, take_columns, axis=1)
    trained_in, trained_out = local_round(
        handed_in, handed_out, pool_inputs, pool_targets, row_picks, STEPS, scale_in, scale_out
    )
    return (trained_in, trained_out, prediction)


def solution(mesh):
    in_specs = (
        P("sub", None),
        P("sub", None),
        P(None, "sub"),
        P(None, "sub"),
        P(None, "sub"),
        P("sub", None),
        P(),
    )
    out_specs = (P(None, "sub"), P(None, "sub"), P("sub", None))
    return jax.shard_map(
        per_device, mesh=mesh, in_specs=in_specs, out_specs=out_specs, check_vma=False
    )
```

profile of v0, /device:TPU:1, one launch (start us, length us, event | category | flops | bytes accessed | tf_op | source)
XLA Modules:
  0.0 1054.3 jit_solution(7046368642467714534)
XLA Ops:
  13.8 15.5 %scatter_custom_fusion = s32[4096]{0:T(1024)S(1)} fusion(s32[4096]{0:T(1024)S(1)} %compare_select_fusion.2, s32[4096]{0:T(1024)S(1)} %iota.16, s32[]{:T(128)} %constant.305.clone.1), kind=kCustom, calls=%fused_computation.142 | custom fusion | bytes 16388 | tf_op jit(solution)/shard_map/scatter | solution.py:89
  30.9 157.9 %while.36 = (s32[]{:T(128)}, f32[4096,256]{1,0:T(8,128)}, f32[4096,256]{1,0:T(8,128)}, s32[8,256]{1,0:T(8,128)}, bf16[512,4096]{1,0:T(8,128)(2,1)}, /*index=5*/bf16[512,4096]{1,0:T(8,128)(2,1)}, s32[]{:T(128)}) while((s32[]{:T(128)}, f32[4096,256]{1,0:T(8,128)}, f32[4096,256]{1,0:T(8,128)}, s32[8,256]{1,0:T(8,128)}, ...), condition=%wide.region_1.3_spmd, body=%wide.region_0.2_spmd.sunk | while | flops 2701724928 | bytes 59782260 | solution.py:56
  31.6 6.6 gather_fusion.1
  42.0 7.9 gather_fusion
  53.7 8.6 fusion.148
  68.1 6.6 gather_fusion.1
  78.5 7.9 gather_fusion
  90.2 8.6 fusion.148
  104.7 6.6 gather_fusion.1
  115.0 7.9 gather_fusion
  126.8 8.6 fusion.148
  151.5 7.9 gather_fusion
  163.3 8.6 fusion.148
  200.2 16.8 %gather_fusion.6 = f32[1024,4096]{1,0:T(8,128)} fusion(f32[4096,256]{0,1:T(8,128)} %copy.23, s32[1024]{0:T(1024)S(1)} %fusion.111), kind=kCustom, calls=%fused_computation.6.clone | custom fusion | bytes 33558528 | tf_op jit(solution)/shard_map/jit(_take)/gather | solution.py:100
  217.0 16.8 %gather_fusion.4 = f32[1024,4096]{1,0:T(8,128)} fusion(f32[4096,256]{0,1:T(8,128)} %copy.22, s32[1024]{0:T(1024)S(1)} %fusion.111), kind=kCustom, calls=%fused_computation.1.clone | custom fusion | bytes 33558528 | tf_op jit(solution)/shard_map/jit(_take)/gather | solution.py:99
  233.8 16.9 %select_bitcast_fusion = (f32[4096,128,8]{0,2,1:T(8,128)S(1)}, f32[4096,128,8]{0,2,1:T(8,128)}) fusion(f32[1024,4096]{1,0:T(8,128)} %gather_fusion.6, pred[1024]{0:T(1024)(128)(4,1)S(1)} %copy-done.4, f32[1024,4096]{1,0:T(8,128)} %gather_fusion.4), kind=kLoop, calls=%fused_computation.117 | loop fusion | flops 8388608 | bytes 67109888 | tf_op jit(solution)/shard_map/all_to_all | solution.py:103
  250.7 199.2 %all_to_all.24 = f32[4096,128,8]{0,2,1:T(8,128)} all-to-all(f32[4096,128,8]{0,2,1:T(8,128)S(1)} %get-tuple-element.425), channel_id=1, replica_groups=mesh['sub'=128] {'sub'}, dimensions={1} | all-to-all | bytes 33554432 | tf_op jit(solution)/shard_map/all_to_all | solution.py:103
  456.4 235.1 %all-gather.3.cloned.1.call-done = bf16[128,2,4096]{2,1,0:T(2,128)(2,1)} async-done(((bf16[1,2,4096]{2,1,0:T(2,128)(2,1)}), bf16[128,2,4096]{2,1,0:T(2,128)(2,1)}) %all-gather.3.cloned.1.call-update) | async-done | bytes 2097168 | tf_op jit(solution)/shard_map/all_gather | solution.py:74
  694.3 8.0 convolution_multiply_fusion.8
  703.1 153.8 %all-reduce.3.cloned.1.call-done = f32[256,4096]{1,0:T(8,128)} async-done(((f32[256,4096]{1,0:T(8,128)}), f32[256,4096]{1,0:T(8,128)}) %all-reduce.3.cloned.1.call-update) | async-done | bytes 4194320
  858.5 11.5 %gather_fusion.7 = f32[256,4096]{1,0:T(8,128)} fusion(f32[4096,1024]{0,1:T(8,128)} %bitcast.47, s32[1024]{0:T(1024)S(1)} %pad_clamp_fusion.2), kind=kCustom, calls=%fused_computation.7.clone | custom fusion | bytes 8389632 | tf_op jit(solution)/shard_map/jit(_take)/gather | solution.py:109
  870.0 11.5 %gather_fusion.5 = f32[256,4096]{1,0:T(8,128)} fusion(f32[4096,1024]{0,1:T(8,128)} %bitcast.4, s32[1024]{0:T(1024)S(1)} %pad_clamp_fusion.2), kind=kCustom, calls=%fused_computation.2.clone | custom fusion | bytes 8389632 | tf_op jit(solution)/shard_map/jit(_take)/gather | solution.py:108
  881.5 8.4 select_bitcast_fusion.2
  901.1 146.0 %while.37 = (s32[]{:T(128)}, f32[4096,256]{1,0:T(8,128)}, f32[4096,256]{1,0:T(8,128)}, s32[8,256]{1,0:T(8,128)}, bf16[512,4096]{1,0:T(8,128)(2,1)}, /*index=5*/b...) while((s32[]{:T(128)}, f32[4096,256]{1,0:T(8,128)}, f32[4096,256]{1,0:T(8,128)}, ...), condition=%wide.region_5.9_spmd, body=%wide.region_4.8_spmd.sunk | while | flops 2701724928 | bytes 59782328 | solution.py:56
  912.2 7.9 gather_fusion.2
  923.9 8.6 fusion.157
  948.7 7.9 gather_fusion.2
  960.4 8.6 fusion.157
  985.2 7.9 gather_fusion.2
  996.9 8.6 fusion.157
  1021.7 7.9 gather_fusion.2
  1033.4 8.6 fusion.157
  (113 shorter events, 181.9 us)
Async XLA Ops:
  7.2 4.6 copy-start.2
  11.8 2.0 copy-start.3
  38.3 3.7 copy-start
  74.8 3.7 copy-start
  111.3 3.7 copy-start
  147.8 3.7 copy-start
  217.0 16.8 %copy-start.4 = (pred[1024]{0:T(1024)(128)(4,1)S(1)}, pred[1024]{0:T(1024)(128)(4,1)}, u32[]{:S(2)}) copy-start(pred[1024]{0:T(1024)(128)(4,1)} %compare_and_fusion.2) | copy-start | bytes 3076
  449.9 420.0 %all-to-all-start = ((f32[4096,128,8]{0,2,1:T(8,128)}), f32[4096,128,8]{0,2,1:T(8,128)}, u32[]{:S(2)}, u32[]{:S(2)}) async-start(f32[4096,128,8]{0,2,1:T(8,128)} %get-tuple-element.426), calls=%async_computation | async-start | bytes 33554432 | tf_op jit(solution)/shard_map/all_to_all | solution.py:102
  455.6 235.9 %all-gather.3.cloned.1.call-start = ((), (), s32[]{:S(2)}) async-start(), calls=%async_computation.2 | async-start | bytes 2113536 | tf_op jit(solution)/shard_map/all_gather | solution.py:74
  456.4 400.6 %all-reduce.3.cloned.1.call-start = ((), (), s32[]{:S(2)}) async-start(), calls=%async_computation.3 | async-start | bytes 8388608
  702.2 0.7 copy-start.5
  908.4 3.7 copy-start.1
  944.9 3.7 copy-start.1
  981.5 3.7 copy-start.1
  1018.0 3.7 copy-start.1
Sparse Core Ops, SparseCore 0:
  459.6 231.8 all-gather.2
  702.4 154.5 all-reduce.2
where the time goes:
time: 1070 us; the launch traced here: 1050 us
  waiting for transfers between devices  390 us (36%)
  local copies, waits for them, and re-layouts  228 us (21%)
  blocking collectives  199 us (19%)
  matrix products  177 us (17%)
  other arithmetic  27 us (3%)
  between operations  14.5 us (1%)
  loops' own time  12.4 us (1%)
    all_gather x1, waiting for transfers between devices, per_device(): lax.all_gather(eval_inputs, 'sub', axis=0, tiled=True)  235 us
    all_to_all x1, blocking collectives, per_device(): lax.all_to_all(outgoing_out, 'sub', split_axis=1, concat_axis=1, tiled=True)  199 us
    unnamed x3, waiting for transfers between devices  155 us
    dot_general x8, matrix products, train_step(): jnp.dot(batch_rows.T, backward, preferred_element_type=jnp.float32)  68.7 us
    gather x8, local copies, waits for them, and re-layouts, one_turn(): batch_goals = jnp.take(pool_targets, picked, axis=0)  63.4 us
    gather x8, local copies, waits for them, and re-layouts, one_turn(): batch_rows = jnp.take(pool_inputs, picked, axis=0)  52.9 us
    dot_general x8, matrix products, train_step(): jnp.dot(errors.T, activity, preferred_element_type=jnp.float32) * scale_out  40.7 us
    dot_general x8, matrix products, train_step(): jnp.dot(activity, out_half.T, preferred_element_type=jnp.float32)  30.4 us
  transfers between devices with their start and end apart: 3, of which 2 were waited for; matrix products, arithmetic and copies ran while one was open for 2% of the time, Pallas kernels for 0%

commit v1 on v0

--- a/solution.py
+++ b/solution.py
@@ -71,7 +71,9 @@
     out_half = layer_out.astype(jnp.bfloat16)
     eval_act = gelu_value(
         jnp.dot(
-            lax.all_gather(eval_inputs, "sub", axis=0, tiled=True),
+            jnp.concatenate(
+                lax.all_to_all(jnp.stack([eval_inputs] * lax.axis_size("sub")), "sub", 0, 0), axis=0
+            ),
             in_half,
             preferred_element_type=jnp.float32,
         )

time: 1070 us -> 1020 us (0.953)
  waiting for transfers between devices: 390 us -> 327 us
  starting transfers between devices: 5.74 us -> 17.7 us
    all_gather x1 -> x0, waiting for transfers between devices: 235 us -> none  [per_device(): lax.all_gather(eval_inputs, 'sub', axis=0, tiled=True)]
    unnamed x3 -> x2, waiting for transfers between devices: 155 us -> 327 us
    all_to_all x0 -> x1, starting transfers between devices: none -> 12 us  [per_device(): lax.all_to_all(jnp.stack([eval_inputs] * lax.axis_size('sub')), 'sub', 0, 0)]
  transfers between devices with their start and end apart: 3 -> 3, of which waited for: 2 -> 1; matrix products, arithmetic and copies ran while one was open for 2% -> 25% of each run, Pallas kernels for 0% -> 0%
where the time goes in v1:
time: 1020 us; the launch traced here: 1010 us
  waiting for transfers between devices  327 us (32%)
  local copies, waits for them, and re-layouts  232 us (23%)
  blocking collectives  198 us (19%)
  matrix products  177 us (17%)
  other arithmetic  31.8 us (3%)
  starting transfers between devices  17.7 us (2%)
  between operations  14.4 us (1%)
  loops' own time  12.7 us (1%)
    unnamed x2, waiting for transfers between devices  327 us
    all_to_all x1, blocking collectives, per_device(): lax.all_to_all(outgoing_out, 'sub', split_axis=1, concat_axis=1, tiled=True)  198 us
    dot_general x8, matrix products, train_step(): jnp.dot(batch_rows.T, backward, preferred_element_type=jnp.float32)  68.7 us
    gather x8, local copies, waits for them, and re-layouts, one_turn(): batch_goals = jnp.take(pool_targets, picked, axis=0)  63.4 us
    gather x8, local copies, waits for them, and re-layouts, one_turn(): batch_rows = jnp.take(pool_inputs, picked, axis=0)  52.9 us
    dot_general x8, matrix products, train_step(): jnp.dot(errors.T, activity, preferred_element_type=jnp.float32) * scale_out  40.7 us
    dot_general x8, matrix products, train_step(): jnp.dot(activity, out_half.T, preferred_element_type=jnp.float32)  30.4 us
    dot_general x8, matrix products, train_step(): jnp.dot(batch_rows, in_half, preferred_element_type=jnp.float32) * scale_in  29.6 us
  transfers between devices with their start and end apart: 3, of which 1 were waited for; matrix products, arithmetic and copies ran while one was open for 25% of the time, Pallas kernels for 0%

profile of v1, /device:TPU:1, one launch (start us, length us, event | category | flops | bytes accessed | tf_op | source)
XLA Modules:
  0.0 1010.3 jit_solution(4689772001606844006)
XLA Ops:
  17.3 12.0 %all-to-all-start.2 = ((bf16[128,2,4096]{2,1,0:T(2,128)(2,1)}), bf16[128,2,4096]{2,1,0:T(2,128)(2,1)}, u32[]{:S(2)}, u32[]{:S(2)}) async-start(bf16[128,2,4096]{2,1,0:T(2,128)(2,1)} %stack.2), calls=%async_computation.2 | async-start | bytes 4194304 | tf_op jit(solution)/shard_map/all_to_all | solution.py:75
  29.3 15.5 %scatter_custom_fusion = s32[4096]{0:T(1024)S(1)} fusion(s32[4096]{0:T(1024)S(1)} %compare_select_fusion.2, s32[4096]{0:T(1024)S(1)} %iota.16, s32[]{:T(128)} %constant.305.clone.1), kind=kCustom, calls=%fused_computation.142 | custom fusion | bytes 16388 | tf_op jit(solution)/shard_map/scatter | solution.py:91
  46.4 158.3 %while.36 = (s32[]{:T(128)}, f32[4096,256]{1,0:T(8,128)}, f32[4096,256]{1,0:T(8,128)}, s32[8,256]{1,0:T(8,128)}, bf16[512,4096]{1,0:T(8,128)(2,1)}, /*index=5*/bf16[512,4096]{1,0:T(8,128)(2,1)}, s32[]{:T(128)}) while((s32[]{:T(128)}, f32[4096,256]{1,0:T(8,128)}, f32[4096,256]{1,0:T(8,128)}, s32[8,256]{1,0:T(8,128)}, ...), condition=%wide.region_1.3_spmd, body=%wide.region_0.2_spmd.sunk | while | flops 2701724928 | bytes 59782260 | solution.py:56
  47.5 6.6 gather_fusion.1
  57.8 7.9 gather_fusion
  69.5 8.6 fusion.148
  94.3 7.9 gather_fusion
  106.0 8.6 fusion.148
  120.5 6.6 gather_fusion.1
  130.8 7.9 gather_fusion
  142.6 8.6 fusion.148
  157.0 6.6 gather_fusion.1
  167.3 7.9 gather_fusion
  179.1 8.6 fusion.148
  215.9 16.8 %gather_fusion.6 = f32[1024,4096]{1,0:T(8,128)} fusion(f32[4096,256]{0,1:T(8,128)} %copy.23, s32[1024]{0:T(1024)S(1)} %fusion.111), kind=kCustom, calls=%fused_computation.6.clone | custom fusion | bytes 33558528 | tf_op jit(solution)/shard_map/jit(_take)/gather | solution.py:102
  232.8 16.8 %gather_fusion.4 = f32[1024,4096]{1,0:T(8,128)} fusion(f32[4096,256]{0,1:T(8,128)} %copy.22, s32[1024]{0:T(1024)S(1)} %fusion.111), kind=kCustom, calls=%fused_computation.1.clone | custom fusion | bytes 33558528 | tf_op jit(solution)/shard_map/jit(_take)/gather | solution.py:101
  249.6 21.7 %select_bitcast_fusion = (f32[4096,128,8]{0,2,1:T(8,128)}, f32[4096,128,8]{0,2,1:T(8,128)}) fusion(f32[1024,4096]{1,0:T(8,128)} %gather_fusion.6, pred[1024]{0:T(1024)(128)(4,1)S(1)} %copy-done.5, f32[1024,4096]{1,0:T(8,128)} %gather_fusion.4), kind=kLoop, calls=%fused_computation.117 | loop fusion | flops 8388608 | bytes 67109888 | tf_op jit(solution)/shard_map/all_to_all | solution.py:105
  271.3 197.7 %all_to_all.29 = f32[4096,128,8]{0,2,1:T(8,128)} all-to-all(f32[4096,128,8]{0,2,1:T(8,128)} %get-tuple-element.425), channel_id=1, replica_groups=mesh['sub'=128] {'sub'}, dimensions={1} | all-to-all | bytes 33554432 | tf_op jit(solution)/shard_map/all_to_all | solution.py:105
  477.5 8.0 convolution_multiply_fusion.8
  486.3 326.8 %all-reduce.3.cloned.1.call-done = f32[256,4096]{1,0:T(8,128)} async-done(((f32[256,4096]{1,0:T(8,128)}), f32[256,4096]{1,0:T(8,128)}) %all-reduce.3.cloned.1.call-update) | async-done | bytes 4194320
  814.6 11.5 %gather_fusion.7 = f32[256,4096]{1,0:T(8,128)} fusion(f32[4096,1024]{0,1:T(8,128)} %bitcast.46, s32[1024]{0:T(1024)S(1)} %pad_clamp_fusion.2), kind=kCustom, calls=%fused_computation.7.clone | custom fusion | bytes 8389632 | tf_op jit(solution)/shard_map/jit(_take)/gather | solution.py:111
  826.1 11.5 %gather_fusion.5 = f32[256,4096]{1,0:T(8,128)} fusion(f32[4096,1024]{0,1:T(8,128)} %bitcast.4, s32[1024]{0:T(1024)S(1)} %pad_clamp_fusion.2), kind=kCustom, calls=%fused_computation.2.clone | custom fusion | bytes 8389632 | tf_op jit(solution)/shard_map/jit(_take)/gather | solution.py:110
  837.6 8.4 select_bitcast_fusion.2
  857.2 146.0 %while.37 = (s32[]{:T(128)}, f32[4096,256]{1,0:T(8,128)}, f32[4096,256]{1,0:T(8,128)}, s32[8,256]{1,0:T(8,128)}, bf16[512,4096]{1,0:T(8,128)(2,1)}, /*index=5*/b...) while((s32[]{:T(128)}, f32[4096,256]{1,0:T(8,128)}, f32[4096,256]{1,0:T(8,128)}, ...), condition=%wide.region_5.9_spmd, body=%wide.region_4.8_spmd.sunk | while | flops 2701724928 | bytes 59782328 | solution.py:56
  868.3 7.9 gather_fusion.2
  880.0 8.6 fusion.157
  904.8 7.9 gather_fusion.2
  916.5 8.6 fusion.157
  941.3 7.9 gather_fusion.2
  953.0 8.6 fusion.157
  977.8 7.9 gather_fusion.2
  989.5 8.6 fusion.157
  (115 shorter events, 184.6 us)
Async XLA Ops:
  7.2 4.6 copy-start.2
  11.8 2.0 copy-start.4
  13.8 15.4 %copy-start.3 = (s32[4096]{0:T(1024)S(1)}, s32[4096]{0:T(1024)}, u32[]{:S(2)}) copy-start(s32[4096]{0:T(1024)} %param.23) | copy-start | bytes 49156
  17.3 254.0 %all-to-all-start.2 = ((bf16[128,2,4096]{2,1,0:T(2,128)(2,1)}), bf16[128,2,4096]{2,1,0:T(2,128)(2,1)}, u32[]{:S(2)}, u32[]{:S(2)}) async-start(bf16[128,2,4096]{2,1,0:T(2,128)(2,1)} %stack.2), calls=%async_computation.2 | async-start | bytes 4194304 | tf_op jit(solution)/shard_map/all_to_all | solution.py:75
  54.1 3.7 copy-start
  90.6 3.7 copy-start
  127.1 3.7 copy-start
  163.6 3.7 copy-start
  232.8 16.8 %copy-start.5 = (pred[1024]{0:T(1024)(128)(4,1)S(1)}, pred[1024]{0:T(1024)(128)(4,1)}, u32[]{:S(2)}) copy-start(pred[1024]{0:T(1024)(128)(4,1)} %compare_and_fusion.2) | copy-start | bytes 3076
  469.0 357.1 %all-to-all-start = ((f32[4096,128,8]{0,2,1:T(8,128)}), f32[4096,128,8]{0,2,1:T(8,128)}, u32[]{:S(2)}, u32[]{:S(2)}) async-start(f32[4096,128,8]{0,2,1:T(8,128)} %get-tuple-element.426), calls=%async_computation | async-start | bytes 33554432 | tf_op jit(solution)/shard_map/all_to_all | solution.py:104
  474.7 338.4 %all-reduce.3.cloned.1.call-start = ((), (), s32[]{:S(2)}) async-start(), calls=%async_computation.3 | async-start | bytes 8388608
  485.4 0.7 copy-start.6
  864.5 3.7 copy-start.1
  901.0 3.7 copy-start.1
  937.5 3.7 copy-start.1
  974.0 3.7 copy-start.1
Sparse Core Ops, SparseCore 0:
  485.6 327.4 all-reduce.2
